TPU v7x, 512 devices: a whole 4x8x8 slice. The times are simulated.
512 devices in a mesh: tiles: 128 (over z, y, core), rep: 4 (over x).
Axes of the slice: x: 4, y: 8, z: 8, core: 2. Of those that a mesh axis runs over, the one named last changes fastest.
Arguments:
- tile_data: float32 [1536, 64, 4096], P(('tiles', 'rep')), may hold values from -64 to 64
- tile_coords: int32 [1536, 3], P(('tiles', 'rep')), may hold values from 0 to 127, as said below
- tile_count: int32 [512], P(('tiles', 'rep')), may hold values from 1 to 3, 1024 in all
- weights: int32 [1536], P(('tiles', 'rep')), may hold values from 1 to 4
- owner_map: int32 [128], replicated, may hold values from 0 to 127, as said below
- factor_b: bfloat16 [8192, 256], P(('tiles', 'rep'))
- factor_c: bfloat16 [1024, 256], replicated
Outputs:
- updated: float32 [8192, 256], P(('tiles', 'rep'))
Inputs may be any that keep to these rules, and one draw needn't show every extreme that they name: `tile_coords`: columns 0 and 1 name row blocks below 128, column 2 a block below 16. Every slot of device d = t * 4 + e has owner_map[i_s] = t. Among the 3 slots of one device the positions owner_map[j_s] all differ. `owner_map`: A permutation of the 128 row blocks.
All inputs are finite; a program needn't handle non-finite values. No bound on the sum of `tile_count` on one device may be relied on, other than what follows from the above.
Results may differ from a plain program's by a relative error of at most 0.0095.
Values may be sent and summed in bfloat16 or wider, within the bound.
No kernel may reach another device: no remote copies, remote signals or barrier semaphores. Data moves between devices by JAX's collectives and lax.ppermute only.
A program may use at most 128 MiB of HBM per device.

v0:
```python
import jax
import jax.numpy as jnp
from jax import lax
from jax.sharding import PartitionSpec as P


def per_device(tile_data, tile_coords, tile_count, weights, owner_map, factor_b, factor_c):
    slot_total = tile_data.shape[0]
    tile_edge = tile_data.shape[1]
    rank_cols = factor_b.shape[1]
    is_live = jnp.arange(slot_total, dtype=jnp.int32) < tile_count[0]
    slot_scale = weights.astype(jnp.float32) * is_live.astype(jnp.float32)
    stored_second = jnp.take(owner_map, tile_coords[:, 1])
    block_offsets = jnp.arange(tile_edge, dtype=jnp.int32)
    initial = jnp.zeros((slot_total, tile_edge, rank_cols), jnp.bfloat16)
    owned = lax.all_gather(factor_b, "rep", axis=0, tiled=True)
    row_piece = lax.all_gather(owned, "tiles", axis=0, tiled=True)
    piece_rows = row_piece.shape[0]
    wanted = stored_second[:, None] * tile_edge + block_offsets[None, :]
    inside = (wanted >= 0) & (wanted < piece_rows)
    taken = jnp.take(row_piece, jnp.clip(wanted, 0, piece_rows - 1), axis=0)
    blocks = jnp.where(inside[:, :, None], taken, initial)
    summed = jnp.zeros((tile_edge, rank_cols), jnp.float32)
    for position in range(slot_total):
        c_block = lax.dynamic_slice_in_dim(
            factor_c, tile_coords[position, 2] * tile_edge, tile_edge, 0
        ).astype(jnp.float32)
        flat_tile = tile_data[position].reshape(tile_edge * tile_edge, tile_edge)
        inner_sum = jnp.dot(flat_tile, c_block, precision=lax.Precision.HIGHEST)
        inner_sum = inner_sum.reshape(tile_edge, tile_edge, rank_cols)
        partial_value = jnp.einsum("ijr,jr->ir", inner_sum, blocks[position].astype(jnp.float32))
        rounded = (partial_value * slot_scale[position]).astype(jnp.bfloat16)
        summed = summed + rounded.astype(jnp.float32)
    my_rows = lax.psum_scatter(summed, "rep", scatter_dimension=0, tiled=True)
    own_gram = jnp.dot(factor_b.T, factor_b, preferred_element_type=jnp.float32)
    gram_b = lax.psum(own_gram, ("tiles", "rep"))
    gram_c = jnp.dot(factor_c.T, factor_c, preferred_element_type=jnp.float32)
    normal_matrix = gram_b * gram_c
    lower_factor = jnp.linalg.cholesky(normal_matrix)
    return jax.scipy.linalg.cho_solve((lower_factor, True), my_rows.T).T


def solution(mesh):
    in_specs = (
        P(("tiles", "rep"), None, None),
        P(("tiles", "rep"), None),
        P(("tiles", "rep")),
        P(("tiles", "rep")),
        P(),
        P(("tiles", "rep"), None),
        P(),
    )
    out_specs = P(("tiles", "rep"), None)
    return jax.shard_map(
        per_device, mesh=mesh, in_specs=in_specs, out_specs=out_specs, check_vma=False
    )
```

profile of v0, /device:TPU:23, one launch (start us, length us, event | category | flops | bytes accessed | tf_op | source)
XLA Modules:
  0.0 374.4 jit_solution(15148988416922388078)
XLA Ops:
  7.4 1.7 fusion.28
  9.1 10.0 %all_gather.6 = bf16[64,256]{1,0:T(8,128)(2,1)} all-gather(bf16[16,256]{1,0:T(8,128)(2,1)} %param.12), channel_id=1, replica_groups=mesh['tiles'=128,'rep'=4] {'rep'}, dimensions={0}, use_global_device_ids=true | all-gather | bytes 40960 | tf_op jit(solution)/shard_map/all_gather | solution.py:16
  19.2 0.8 slice.101
  19.9 1.5 fusion.26
  23.4 0.1 copy.55
  23.5 1.3 gather_fusion
  25.0 3.7 fusion.25
  28.7 2.0 reshape_squeeze.9
  30.7 3.9 %convolution_bitcast_fusion.2 = f32[4096,256]{0,1:T(8,128)} fusion(f32[4096,64]{1,0:T(8,128)S(1)} %reshape_squeeze.9, bf16[1024,256]{1,0:T(8,128)(2,1)S(1)} %copy-done, s32[]{:T(128)S(6)} %select_n.56), kind=kOutput, calls=%fused_computation.6 | convolution fusion | flops 805306368 | bytes 6324228 | tf_op jit(solution)/shard_map/dot_general | solution.py:29
  34.7 5.6 %copy.50 = f32[4096,256]{1,0:T(8,128)} copy(f32[4096,256]{0,1:T(8,128)} %convolution_bitcast_fusion.2) | data formatting | bytes 8388608
  40.3 2.0 reshape_squeeze.11
  42.3 3.9 %convolution_bitcast_fusion = f32[4096,256]{0,1:T(8,128)} fusion(f32[4096,64]{1,0:T(8,128)S(1)} %reshape_squeeze.11, bf16[1024,256]{1,0:T(8,128)(2,1)S(1)} %copy-done, s32[]{:T(128)S(6)} %select_n.58), kind=kOutput, calls=%fused_computation.4 | convolution fusion | flops 805306368 | bytes 6324228 | tf_op jit(solution)/shard_map/dot_general | solution.py:29
  46.2 5.6 %copy.52 = f32[4096,256]{1,0:T(8,128)} copy(f32[4096,256]{0,1:T(8,128)} %convolution_bitcast_fusion) | data formatting | bytes 8388608
  51.8 2.0 reshape_squeeze.10
  53.8 3.9 %convolution_bitcast_fusion.1 = f32[4096,256]{0,1:T(8,128)} fusion(f32[4096,64]{1,0:T(8,128)S(1)} %reshape_squeeze.10, bf16[1024,256]{1,0:T(8,128)(2,1)S(1)} %copy-done, s32[]{:T(128)S(6)} %select_n.57), kind=kOutput, calls=%fused_computation.5 | convolution fusion | flops 805306368 | bytes 6324228 | tf_op jit(solution)/shard_map/dot_general | solution.py:29
  57.7 5.7 %copy.51 = f32[4096,256]{1,0:T(8,128)} copy(f32[4096,256]{0,1:T(8,128)} %convolution_bitcast_fusion.1) | data formatting | bytes 8388608
  64.1 0.7 fusion.27
  64.8 223.5 %all-reduce.3.cloned.1.call-done = f32[256,256]{0,1:T(8,128)} async-done(((f32[256,256]{0,1:T(8,128)}), f32[256,256]{0,1:T(8,128)}) %all-reduce.3.cloned.1.call-update) | async-done | bytes 262160 | tf_op jit(solution)/shard_map/psum | solution.py:36
  288.3 1.3 convolution_multiply_fusion
  289.6 0.1 copy.21
  289.8 11.7 %cholesky.50 = f32[128,128]{1,0:T(8,128)S(1)} custom-call(f32[128,128]{1,0:T(8,128)S(1)} %cholesky.118), custom_call_target="Cholesky" | custom-call | tf_op jit(solution)/shard_map/jit(cholesky)/cholesky | solution.py:39
  301.5 9.8 %custom-call.18 = f32[1,128,128]{1,2,0:T(8,128)S(1)} custom-call(f32[1,128,128]{2,1,0:T(8,128)S(1)} %get-tuple-element.32), custom_call_target="InvertDiagBlocksLowerTriangular" | custom-call | tf_op jit(solution)/shard_map/jit(cholesky)/cholesky | solution.py:39
  311.4 0.2 constant_dynamic-update-slice_fusion
  311.6 0.3 convolution_subtract_fusion
  311.8 11.7 %cholesky.105 = f32[128,128]{1,0:T(8,128)S(1)} custom-call(f32[128,128]{1,0:T(8,128)S(1)} %convolution_subtract_fusion), custom_call_target="Cholesky" | custom-call | tf_op jit(solution)/shard_map/jit(cholesky)/cholesky | solution.py:39
  323.6 0.7 compare_reduce_fusion
  325.6 3.6 gather_fusion.1
  329.2 0.1 select_select_fusion.1
  329.3 3.0 multiply_reduce_fusion.2
  332.4 0.1 copy.35
  332.5 4.9 %multiply_reduce_fusion = (f32[256,64]{0,1:T(8,128)S(1)}, f32[256,64]{0,1:T(8,128)S(1)}) fusion(f32[256,64]{0,1:T(8,128)S(1)} %get-tuple-element.26, f32[4096,256]{1,0:T(8,128)} %copy.52, f32[4096,256]{1,0:T(8,128)} %copy.51, f32[256,64]{0,1:T(8,128)S(1)} %get-tuple-element.27), kind=kLoop, calls=%fused_computation.7 | loop fusion | flops 4161536 | bytes 8650752
  337.4 0.1 copy.42
  337.5 0.1 copy.49
  337.6 1.9 add_bitcast_fusion
  339.5 0.7 copy.53
  340.3 3.8 %while.1 = (s32[]{:T(128)}, f32[256,256]{1,0:T(8,128)S(1)}, s32[2,2]{1,0:T(2,128)S(1)}, f32[2,128,128]{2,1,0:T(8,128)S(1)}, s32[]{:T(128)}) while((s32[]{:T(128)}, f32[256,256]{1,0:T(8,128)S(1)}, s32[2,2]{1,0:T(2,128)S(1)}, f32[2,128,128]{2,1,0:T(8,128)S(1)}, s32[]{:T(128)}) %tuple.33), condition=%wide.while_cond, body=%wide.while_body.sunk | while | flops 2 | bytes 131189 | solution.py:40
  340.3 0.6 fusion.44
  340.9 1.3 bitcast_dynamic-update-slice_fusion.2
  342.2 0.6 fusion.44
  342.8 1.3 bitcast_dynamic-update-slice_fusion.2
  344.1 19.7 %custom-call.19 = f32[2,128,128]{1,2,0:T(8,128)S(1)} custom-call(f32[2,128,128]{2,1,0:T(8,128)S(1)} %get-tuple-element.12), custom_call_target="InvertDiagBlocksLowerTriangular" | custom-call | tf_op jit(solution)/shard_map/jit(_cho_solve)/triangular_solve | solution.py:40
  363.8 0.9 fusion.5
  364.7 0.9 convolution_subtract_fusion.2
  365.5 0.2 fusion.7
  365.7 0.2 fusion.6
  365.9 0.2 convolution_subtract_fusion.1
  366.1 0.2 fusion.4
  366.3 0.7 maximum_bitcast_fusion
  (32 shorter events, 0.7 us)
Async XLA Ops:
  7.4 23.4 %copy-start = (bf16[1024,256]{1,0:T(8,128)(2,1)S(1)}, bf16[1024,256]{1,0:T(8,128)(2,1)}, u32[]{:S(2)}) copy-start(bf16[1024,256]{1,0:T(8,128)(2,1)} %param.13) | copy-start | bytes 1572868
  7.4 280.9 %all-reduce.3.cloned.1.call-start = ((), (), s32[]{:S(2)}) async-start(), calls=%async_computation.1 | async-start | bytes 524288 | tf_op jit(solution)/shard_map/psum | solution.py:36
  9.1 316.5 %all-gather.2.cloned.1.call-start = ((), (), s32[]{:S(2)}) async-start(), calls=%async_computation.2 | async-start | bytes 4227072 | tf_op jit(solution)/shard_map/all_gather | solution.py:17
  19.1 344.7 %reduce-scatter.4.cloned.1.call-start = ((), (), s32[]{:S(2)}) async-start(), calls=%async_computation.3 | async-start | bytes 81920 | tf_op jit(solution)/shard_map/reduce_scatter | solution.py:34
  57.7 6.3 %copy-start.1 = (s32[3]{0:T(128)S(1)}, s32[3]{0:T(128)}, u32[]{:S(2)}) copy-start(s32[3]{0:T(128)} %param.10) | copy-start | bytes 40
Sparse Core Ops, SparseCore 0:
  13.2 275.0 all-reduce.2
Sparse Core Ops, SparseCore 1:
  19.2 92.1 all-gather.1
  340.3 17.2 reduce-scatter.3
where the time goes:
time: 375 us; the launch traced here: 374 us
  waiting for transfers between devices  224 us (60%)
  other arithmetic  64.6 us (17%)
  local copies, waits for them, and re-layouts  39.5 us (11%)
  between operations  19 us (5%)
  matrix products  17.7 us (5%)
  blocking collectives  9.96 us (3%)
    psum x1, waiting for transfers between devices, per_device(): gram_b = lax.psum(own_gram, ('tiles', 'rep'))  223 us
    another operation x6, other arithmetic, per_device(): lower_factor = jnp.linalg.cholesky(normal_matrix)  34 us
    another operation x3, other arithmetic, per_device(): return jax.scipy.linalg.cho_solve((lower_factor, True), my_rows.T).T  19.7 us
    unnamed x9, local copies, waits for them, and re-layouts  17.7 us
    dot_general x3, matrix products, per_device(): inner_sum = jnp.dot(flat_tile, c_block, precision=lax.Precision.HIGHEST)  11.7 us
    all_gather x1, blocking collectives, per_device(): owned = lax.all_gather(factor_b, 'rep', axis=0, tiled=True)  9.96 us
    unnamed x4, other arithmetic  7.99 us
  transfers between devices with their start and end apart: 3, of which 1 were waited for; matrix products, arithmetic and copies ran while one was open for 27% of the time, Pallas kernels for 0%

commit v1 on v0

--- a/solution.py
+++ b/solution.py
@@ -2,6 +2,12 @@
 import jax.numpy as jnp
 from jax import lax
 from jax.sharding import PartitionSpec as P
+
+
+def joined_along(blocks, dim):
+    shape = list(blocks.shape[1:])
+    shape[dim] *= blocks.shape[0]
+    return jnp.moveaxis(blocks, 0, dim).reshape(shape)
 
 
 def per_device(tile_data, tile_coords, tile_count, weights, owner_map, factor_b, factor_c):
@@ -13,7 +19,19 @@
     stored_second = jnp.take(owner_map, tile_coords[:, 1])
     block_offsets = jnp.arange(tile_edge, dtype=jnp.int32)
     initial = jnp.zeros((slot_total, tile_edge, rank_cols), jnp.bfloat16)
-    owned = lax.all_gather(factor_b, "rep", axis=0, tiled=True)
+    peers = lax.axis_size("rep")
+    pairs = [(i, (i + 1) % peers) for i in range(peers)]
+    back = [(b, a) for a, b in pairs]
+    lower, upper = ([], [])
+    for hop in range(peers - 1):
+        if hop % 2 == 0:
+            lower.append(lax.ppermute(lower[-1] if lower else factor_b, "rep", pairs))
+        else:
+            upper.append(lax.ppermute(upper[-1] if upper else factor_b, "rep", back))
+    blocks_2 = jnp.stack([*lower[::-1], factor_b, *upper])
+    shift = lax.axis_index("rep") - len(lower)
+    blocks_2 = blocks_2[(jnp.arange(peers) - shift) % peers]
+    owned = joined_along(blocks_2, 0)
     row_piece = lax.all_gather(owned, "tiles", axis=0, tiled=True)
     piece_rows = row_piece.shape[0]
     wanted = stored_second[:, None] * tile_edge + block_offsets[None, :]

time: 375 us -> 377 us (level)
  starting transfers between devices: 0.09 us -> 10.7 us
  blocking collectives: 9.96 us -> 0 us
    ppermute x0 -> x3, starting transfers between devices: none -> 10.6 us  [the longest x2 8.06 us: per_device(): lower.append(lax.ppermute(lower[-1] if lower else factor_b, 'rep', pairs))]
    all_gather x1 -> x0, blocking collectives: 9.96 us -> none  [per_device(): owned = lax.all_gather(factor_b, 'rep', axis=0, tiled=True)]
  transfers between devices with their start and end apart: 3 -> 6, of which waited for: 1 -> 2; matrix products, arithmetic and copies ran while one was open for 27% -> 28% of each run, Pallas kernels for 0% -> 0%
where the time goes in v1:
time: 377 us
  waiting for transfers between devices  223 us (59%)
  other arithmetic  65.3 us (17%)
  local copies, waits for them, and re-layouts  40.7 us (11%)
  between operations  19.1 us (5%)
  matrix products  17.6 us (5%)
  starting transfers between devices  10.7 us (3%)
    psum x1, waiting for transfers between devices, per_device(): gram_b = lax.psum(own_gram, ('tiles', 'rep'))  222 us
    another operation x6, other arithmetic, per_device(): lower_factor = jnp.linalg.cholesky(normal_matrix)  34 us
    another operation x3, other arithmetic, per_device(): return jax.scipy.linalg.cho_solve((lower_factor, True), my_rows.T).T  19.7 us
    unnamed x9, local copies, waits for them, and re-layouts  17.7 us
    dot_general x3, matrix products, per_device(): inner_sum = jnp.dot(flat_tile, c_block, precision=lax.Precision.HIGHEST)  11.7 us
    ppermute x2, starting transfers between devices, per_device(): lower.append(lax.ppermute(lower[-1] if lower else factor_b, 'rep', pairs))  8.06 us
    unnamed x4, other arithmetic  7.99 us
  transfers between devices with their start and end apart: 6, of which 2 were waited for; matrix products, arithmetic and copies ran while one was open for 28% of the time, Pallas kernels for 0%

profile of v1, /device:TPU:23, one launch (start us, length us, event | category | flops | bytes accessed | tf_op | source)
XLA Modules:
  0.0 376.5 jit_solution(17185260218224212865)
XLA Ops:
  7.4 2.6 collective-permute-start.2
  10.0 4.0 %collective-permute-start = (bf16[16,256]{1,0:T(8,128)(2,1)}, bf16[16,256]{1,0:T(8,128)(2,1)S(1)}, u32[]{:S(2)}, u32[]{:S(2)}) collective-permute-start(bf16[16,256]{1,0:T(8,128)(2,1)} %param.12), channel_id=1, source_target_pairs={{0,1},{1,2},{2,3},{3,0},{4,5},{5,6},{6,7},{7,4},{8,9},{9,10},{10,1... | collective-permute-start | bytes 24584 | tf_op jit(solution)/shard_map/ppermute | solution.py:28
  14.0 1.7 fusion.30
  15.8 4.0 %collective-permute-start.1 = (bf16[16,256]{1,0:T(8,128)(2,1)S(1)}, bf16[16,256]{1,0:T(8,128)(2,1)S(1)}, u32[]{:S(2)}, u32[]{:S(2)}) collective-permute-start(bf16[16,256]{1,0:T(8,128)(2,1)S(1)} %collective-permute-done), channel_id=1, source_target_pairs={{0,1},{1,2},{2,3},{3,0},{4,5},{5,6},{6,7},{7,4},{8,9},{9,10},{10,1... | collective-permute-start | bytes 24584 | tf_op jit(solution)/shard_map/ppermute | solution.py:28
  19.8 0.7 collective-permute-done.1
  20.6 0.7 pad_maximum_fusion
  21.3 1.1 gather_fusion.1
  22.5 0.8 slice.101
  23.3 1.5 fusion.28
  26.9 1.3 gather_fusion
  28.3 3.7 fusion.27
  32.0 2.0 reshape_squeeze.9
  34.1 3.9 %convolution_bitcast_fusion.2 = f32[4096,256]{0,1:T(8,128)} fusion(f32[4096,64]{1,0:T(8,128)S(1)} %reshape_squeeze.9, bf16[1024,256]{1,0:T(8,128)(2,1)S(1)} %copy-done, s32[]{:T(128)S(6)} %select_n.82), kind=kOutput, calls=%fused_computation.7 | convolution fusion | flops 805306368 | bytes 6324228 | tf_op jit(solution)/shard_map/dot_general | solution.py:47
  38.0 5.6 %copy.50 = f32[4096,256]{1,0:T(8,128)} copy(f32[4096,256]{0,1:T(8,128)} %convolution_bitcast_fusion.2) | data formatting | bytes 8388608
  43.6 2.0 reshape_squeeze.11
  45.6 3.9 %convolution_bitcast_fusion = f32[4096,256]{0,1:T(8,128)} fusion(f32[4096,64]{1,0:T(8,128)S(1)} %reshape_squeeze.11, bf16[1024,256]{1,0:T(8,128)(2,1)S(1)} %copy-done, s32[]{:T(128)S(6)} %select_n.84), kind=kOutput, calls=%fused_computation.5 | convolution fusion | flops 805306368 | bytes 6324228 | tf_op jit(solution)/shard_map/dot_general | solution.py:47
  49.5 5.6 %copy.52 = f32[4096,256]{1,0:T(8,128)} copy(f32[4096,256]{0,1:T(8,128)} %convolution_bitcast_fusion) | data formatting | bytes 8388608
  55.1 2.0 reshape_squeeze.10
  57.1 3.9 %convolution_bitcast_fusion.1 = f32[4096,256]{0,1:T(8,128)} fusion(f32[4096,64]{1,0:T(8,128)S(1)} %reshape_squeeze.10, bf16[1024,256]{1,0:T(8,128)(2,1)S(1)} %copy-done, s32[]{:T(128)S(6)} %select_n.83), kind=kOutput, calls=%fused_computation.6 | convolution fusion | flops 805306368 | bytes 6324228 | tf_op jit(solution)/shard_map/dot_general | solution.py:47
  61.0 5.7 %copy.51 = f32[4096,256]{1,0:T(8,128)} copy(f32[4096,256]{0,1:T(8,128)} %convolution_bitcast_fusion.1) | data formatting | bytes 8388608
  67.4 0.7 fusion.29
  68.1 222.2 %all-reduce.3.cloned.1.call-done = f32[256,256]{0,1:T(8,128)} async-done(((f32[256,256]{0,1:T(8,128)}), f32[256,256]{0,1:T(8,128)}) %all-reduce.3.cloned.1.call-update) | async-done | bytes 262160 | tf_op jit(solution)/shard_map/psum | solution.py:54
  290.4 1.3 convolution_multiply_fusion
  291.7 0.1 copy.21
  291.9 11.7 %cholesky.50 = f32[128,128]{1,0:T(8,128)S(1)} custom-call(f32[128,128]{1,0:T(8,128)S(1)} %cholesky.118), custom_call_target="Cholesky" | custom-call | tf_op jit(solution)/shard_map/jit(cholesky)/cholesky | solution.py:57
  303.6 9.8 %custom-call.18 = f32[1,128,128]{1,2,0:T(8,128)S(1)} custom-call(f32[1,128,128]{2,1,0:T(8,128)S(1)} %get-tuple-element.32), custom_call_target="InvertDiagBlocksLowerTriangular" | custom-call | tf_op jit(solution)/shard_map/jit(cholesky)/cholesky | solution.py:57
  313.4 0.2 constant_dynamic-update-slice_fusion
  313.7 0.3 convolution_subtract_fusion
  313.9 11.7 %cholesky.105 = f32[128,128]{1,0:T(8,128)S(1)} custom-call(f32[128,128]{1,0:T(8,128)S(1)} %convolution_subtract_fusion), custom_call_target="Cholesky" | custom-call | tf_op jit(solution)/shard_map/jit(cholesky)/cholesky | solution.py:57
  325.7 0.7 compare_reduce_fusion
  327.7 3.6 gather_fusion.2
  331.4 3.0 multiply_reduce_fusion.2
  334.6 4.9 %multiply_reduce_fusion = (f32[256,64]{0,1:T(8,128)S(1)}, f32[256,64]{0,1:T(8,128)S(1)}) fusion(f32[256,64]{0,1:T(8,128)S(1)} %get-tuple-element.26, f32[4096,256]{1,0:T(8,128)} %copy.52, f32[4096,256]{1,0:T(8,128)} %copy.51, f32[256,64]{0,1:T(8,128)S(1)} %get-tuple-element.27), kind=kLoop, calls=%fused_computation.8 | loop fusion | flops 4161536 | bytes 8650752
  339.7 1.9 add_bitcast_fusion
  341.6 0.7 copy.53
  342.4 3.8 %while.1 = (s32[]{:T(128)}, f32[256,256]{1,0:T(8,128)S(1)}, s32[2,2]{1,0:T(2,128)S(1)}, f32[2,128,128]{2,1,0:T(8,128)S(1)}, s32[]{:T(128)}) while((s32[]{:T(128)}, f32[256,256]{1,0:T(8,128)S(1)}, s32[2,2]{1,0:T(2,128)S(1)}, f32[2,128,128]{2,1,0:T(8,128)S(1)}, s32[]{:T(128)}) %tuple.33), condition=%wide.while_cond, body=%wide.while_body.sunk | while | flops 2 | bytes 131189 | solution.py:58
  342.4 0.6 fusion.46
  343.0 1.3 bitcast_dynamic-update-slice_fusion.2
  344.3 0.6 fusion.46
  344.9 1.3 bitcast_dynamic-update-slice_fusion.2
  346.2 19.7 %custom-call.19 = f32[2,128,128]{1,2,0:T(8,128)S(1)} custom-call(f32[2,128,128]{2,1,0:T(8,128)S(1)} %get-tuple-element.12), custom_call_target="InvertDiagBlocksLowerTriangular" | custom-call | tf_op jit(solution)/shard_map/jit(_cho_solve)/triangular_solve | solution.py:58
  365.9 0.9 fusion.5
  366.7 0.9 convolution_subtract_fusion.2
  367.6 0.2 fusion.7
  367.8 0.2 fusion.6
  368.0 0.2 convolution_subtract_fusion.1
  368.2 0.2 fusion.4
  368.4 0.7 maximum_bitcast_fusion
  (41 shorter events, 1.3 us)
Async XLA Ops:
  7.4 26.7 %copy-start = (bf16[1024,256]{1,0:T(8,128)(2,1)S(1)}, bf16[1024,256]{1,0:T(8,128)(2,1)}, u32[]{:S(2)}) copy-start(bf16[1024,256]{1,0:T(8,128)(2,1)} %param.13) | copy-start | bytes 1572868
  7.4 283.0 %all-reduce.3.cloned.1.call-start = ((), (), s32[]{:S(2)}) async-start(), calls=%async_computation.1 | async-start | bytes 524288 | tf_op jit(solution)/shard_map/psum | solution.py:54
  7.4 12.5 %collective-permute-start.2 = (bf16[16,256]{1,0:T(8,128)(2,1)}, bf16[16,256]{1,0:T(8,128)(2,1)S(1)}, u32[]{:S(2)}, u32[]{:S(2)}) collective-permute-start(bf16[16,256]{1,0:T(8,128)(2,1)} %param.12), channel_id=1, source_target_pairs={{1,0},{2,1},{3,2},{0,3},{5,4},{6,5},{7,6},{4,7},{9,8},{10,9},{11,1... | collective-permute-start | bytes 24584 | tf_op jit(solution)/shard_map/ppermute | solution.py:30
  10.0 5.8 %collective-permute-start = (bf16[16,256]{1,0:T(8,128)(2,1)}, bf16[16,256]{1,0:T(8,128)(2,1)S(1)}, u32[]{:S(2)}, u32[]{:S(2)}) collective-permute-start(bf16[16,256]{1,0:T(8,128)(2,1)} %param.12), channel_id=1, source_target_pairs={{0,1},{1,2},{2,3},{3,0},{4,5},{5,6},{6,7},{7,4},{8,9},{9,10},{10,1... | collective-permute-start | bytes 24584 | tf_op jit(solution)/shard_map/ppermute | solution.py:28
  15.7 312.0 %all-gather.2.cloned.1.call-start = ((), (), s32[]{:S(2)}) async-start(), calls=%async_computation.2 | async-start | bytes 4227072 | tf_op jit(solution)/shard_map/all_gather | solution.py:35
  15.8 4.8 %collective-permute-start.1 = (bf16[16,256]{1,0:T(8,128)(2,1)S(1)}, bf16[16,256]{1,0:T(8,128)(2,1)S(1)}, u32[]{:S(2)}, u32[]{:S(2)}) collective-permute-start(bf16[16,256]{1,0:T(8,128)(2,1)S(1)} %collective-permute-done), channel_id=1, source_target_pairs={{0,1},{1,2},{2,3},{3,0},{4,5},{5,6},{6,7},{7,4},{8,9},{9,10},{10,1... | collective-permute-start | bytes 24584 | tf_op jit(solution)/shard_map/ppermute | solution.py:28
  22.5 343.4 %reduce-scatter.4.cloned.1.call-start = ((), (), s32[]{:S(2)}) async-start(), calls=%async_computation.3 | async-start | bytes 81920 | tf_op jit(solution)/shard_map/reduce_scatter | solution.py:52
  61.0 6.3 %copy-start.1 = (s32[3]{0:T(128)S(1)}, s32[3]{0:T(128)}, u32[]{:S(2)}) copy-start(s32[3]{0:T(128)} %param.10) | copy-start | bytes 40
Sparse Core Ops, SparseCore 0:
  15.8 274.4 all-reduce.2
Sparse Core Ops, SparseCore 1:
  22.5 92.4 all-gather.1
  342.4 17.2 reduce-scatter.3
